TPU v7x, 512 devices: a whole 4x4x16 slice. The times are simulated.
512 devices in a mesh: band: 32 (over y, x, z_hi), slab: 16 (over z_lo, core).
Axes of the slice: x: 4, y: 4, z: 16 (z_hi: 2, z_lo: 8; z = z_hi * 8 + z_lo), core: 2. Of those that a mesh axis runs over, the one named last changes fastest.
Arguments:
- wave_coeffs: float32 [64, 2, 128, 128, 128], P('band', None, 'slab'), may hold values from -12 to 12
- column_mask: int32 [128, 128], replicated, may hold values from 0 to 1, as said below
- occupations: float32 [64], P('band'), may hold values from 0.1 to 2
- core_density: float32 [128, 128, 128], P('band', 'slab'), may hold values from 0.05 to 0.5
Outputs:
- hartree: float32 [128, 128, 128], P('band', 'slab')
- xc_potential: float32 [128, 128, 128], P('band', 'slab')
Inputs may be any that keep to these rules, and one draw needn't show every extreme that they name: `column_mask`: 1 marks a column of frequencies (first two indices) inside the cutoff; only columns whose shifted indices s1, s2 satisfy s1^2 + s2^2 <= 32^2 can be 1.
All inputs are finite; a program needn't handle non-finite values.
Results may differ from a plain program's by a relative error of at most 0.00035.
Values sent between devices are 32-bit elements; how exact they have to be, the bound alone decides.
No kernel may reach another device: no remote copies, remote signals or barrier semaphores. Data moves between devices by JAX's collectives and lax.ppermute only.
A program may use at most 64 MiB of HBM per device.

v0:
```python
import math
import jax
import jax.numpy as jnp
from jax import lax
from jax.sharding import PartitionSpec as P

grid_spacing = 0.59
wigner_a = 0.44
wigner_b = 7.8


def dft_tables(extent):
    indices = jnp.arange(extent, dtype=jnp.int32)
    phase = indices[:, None] * indices[None, :] % extent
    angle = phase.astype(jnp.float32) * (2.0 * math.pi / extent)
    return (jnp.cos(angle), jnp.sin(angle))


def kernel_block(extent, starts, amounts):
    pieces = []
    for offset, amount in zip(starts, amounts):
        frequency = offset + jnp.arange(amount, dtype=jnp.int32)
        shifted = (frequency + extent // 2) % extent - extent // 2
        pieces.append(shifted * shifted)
    squared = pieces[0][:, None, None] + pieces[1][None, :, None] + pieces[2][None, None, :]
    length = extent * grid_spacing
    scaled = length * length / math.pi / jnp.maximum(squared, 1).astype(jnp.float32)
    return jnp.where(squared == 0, 0.0, scaled)


def exchange_correlation(density):
    root_density = jnp.cbrt(density)
    radius = (3.0 / (4.0 * math.pi)) ** (1.0 / 3.0) / root_density
    exchange_part = -((3.0 / math.pi) ** (1.0 / 3.0)) * root_density
    shifted = radius + wigner_b
    correlation = -wigner_a / shifted - wigner_a * radius / (3.0 * shifted * shifted)
    return exchange_part + correlation


def project(pattern, values, matrix):
    return jnp.einsum(pattern, values, matrix, precision=lax.Precision.HIGHEST)


def rotate(real_part, imag_part, pattern, cosine_table, sine_table, direction):
    new_real = project(pattern, real_part, cosine_table) - direction * project(
        pattern, imag_part, sine_table
    )
    new_imag = direction * project(pattern, real_part, sine_table) + project(
        pattern, imag_part, cosine_table
    )
    return (new_real, new_imag)


def local(wave_coeffs, column_mask, occupations, core_density):
    local_bands = wave_coeffs.shape[0]
    row_count = wave_coeffs.shape[2]
    extent = wave_coeffs.shape[3]
    bands_all = lax.axis_size("band") * local_bands
    band_rows = extent // lax.axis_size("band")
    slab_index = lax.axis_index("slab")
    band_index = lax.axis_index("band")
    cosine_table, sine_table = dft_tables(extent)
    mask_rows = lax.dynamic_slice_in_dim(column_mask, slab_index * row_count, row_count, 0).astype(
        jnp.float32
    )
    masked = wave_coeffs * mask_rows[None, None, :, :, None]
    real_part, imag_part = rotate(
        masked[:, 0], masked[:, 1], "bxyz,zw->bxyw", cosine_table, sine_table, 1.0
    )
    real_part, imag_part = rotate(
        real_part, imag_part, "bxyz,yw->bxwz", cosine_table, sine_table, 1.0
    )
    stacked = jnp.stack((real_part, imag_part), axis=1)
    factor = 1.0 / (float(extent) ** 3 * bands_all)
    partial_value = jnp.zeros((extent, row_count, extent), jnp.float32)
    for member in range(local_bands):
        arrived = lax.all_to_all(stacked[member], "slab", split_axis=2, concat_axis=1, tiled=True)
        plane_real, plane_imag = rotate(
            arrived[0], arrived[1], "xyz,xw->wyz", cosine_table, sine_table, 1.0
        )
        partial_value = partial_value + occupations[member] * (
            plane_real * plane_real + plane_imag * plane_imag
        )
    partial_value = partial_value * factor
    density = lax.psum(partial_value, "band")
    own_density = lax.dynamic_slice_in_dim(density, band_index * band_rows, band_rows, 0)
    first_real = project("xyz,zw->xyw", density, cosine_table)
    first_imag = -project("xyz,zw->xyw", density, sine_table)
    line_real, line_imag = rotate(
        first_real, first_imag, "xyz,xw->wyz", cosine_table, sine_table, -1.0
    )
    arrived = lax.all_to_all(
        jnp.stack((line_real, line_imag)), "slab", split_axis=1, concat_axis=2, tiled=True
    )
    line_real, line_imag = rotate(
        arrived[0], arrived[1], "xyz,yw->xwz", cosine_table, sine_table, -1.0
    )
    kernel = kernel_block(extent, (slab_index * row_count, 0, 0), (row_count, extent, extent))
    line_real, line_imag = rotate(
        kernel * line_real, kernel * line_imag, "xyz,yw->xwz", cosine_table, sine_table, 1.0
    )
    arrived = lax.all_to_all(
        jnp.stack((line_real, line_imag)), "slab", split_axis=2, concat_axis=1, tiled=True
    )
    cosine_rows = lax.dynamic_slice_in_dim(cosine_table, band_index * band_rows, band_rows, 1)
    sine_rows = lax.dynamic_slice_in_dim(sine_table, band_index * band_rows, band_rows, 1)
    line_real, line_imag = rotate(
        arrived[0], arrived[1], "xyz,xw->wyz", cosine_rows, sine_rows, 1.0
    )
    spatial = project("xyz,zw->xyw", line_real, cosine_table) - project(
        "xyz,zw->xyw", line_imag, sine_table
    )
    hartree = spatial / float(extent) ** 3
    xc_potential = exchange_correlation(own_density + core_density)
    return (hartree, xc_potential)


def solution(mesh):
    return jax.shard_map(
        local,
        mesh=mesh,
        in_specs=(P("band", None, "slab", None, None), P(), P("band"), P("band", "slab", None)),
        out_specs=(P("band", "slab", None), P("band", "slab", None)),
        check_vma=False,
    )
```

profile of v0, /device:TPU:65, one launch (start us, length us, event | category | flops | bytes accessed | tf_op | source)
XLA Modules:
  0.0 862.5 jit_solution(3773633972059874277)
XLA Ops:
  7.2 0.7 dynamic-slice_convert_fusion
  7.9 1.9 copy_multiply_fusion
  9.7 1.2 fusion.26
  11.0 1.2 fusion.27
  12.2 1.2 convolution_subtract_fusion.1
  13.4 1.3 fusion.61
  14.7 1.3 fusion.64
  16.0 1.2 convolution_add_fusion.1
  17.2 1.3 fusion.1
  18.6 1.3 fusion
  20.1 1.6 copy.102
  21.7 12.5 %all-to-all-start = ((f32[2,8,128,128]{3,1,0,2:T(8,128)}), f32[2,8,128,128]{3,1,0,2:T(8,128)S(1)}, u32[]{:S(2)}, u32[]{:S(2)}) async-start(f32[2,8,128,128]{3,1,0,2:T(8,128)} %copy.102), calls=%async_computation | async-start | bytes 2097152 | tf_op jit(solution)/shard_map/all_to_all | solution.py:77
  34.2 1.6 copy.104
  35.8 47.0 %all-to-all-done = f32[2,8,128,128]{3,1,0,2:T(8,128)S(1)} async-done(((f32[2,8,128,128]{3,1,0,2:T(8,128)}), f32[2,8,128,128]{3,1,0,2:T(8,128)S(1)}, u32[]{:S(2)}, u32[]{:S(2)}) %all-to-all-start) | async-done | bytes 1048608 | tf_op jit(solution)/shard_map/all_to_all | solution.py:77
  82.8 6.7 all-to-all-start.1
  89.7 0.6 fusion.273
  90.4 0.8 fusion.32
  91.2 0.8 fusion.31
  92.1 46.0 %all-to-all-done.1 = f32[2,8,128,128]{3,1,0,2:T(8,128)S(1)} async-done(((f32[2,8,128,128]{3,1,0,2:T(8,128)}), f32[2,8,128,128]{3,1,0,2:T(8,128)S(1)}, u32[]{:S(2)}, u32[]{:S(2)}) %all-to-all-start.1) | async-done | bytes 1048608 | tf_op jit(solution)/shard_map/all_to_all | solution.py:77
  138.2 0.8 fusion.34
  139.0 0.8 fusion.33
  139.9 0.9 fusion.16
  140.7 0.9 fusion.20
  141.6 1.6 fusion.19
  143.2 2.4 fusion.21
  145.6 554.2 %all-reduce.2.cloned.1.call-done = f32[128,8,128]{2,0,1:T(8,128)} async-done(((f32[128,8,128]{2,0,1:T(8,128)}), f32[128,8,128]{2,0,1:T(8,128)}) %all-reduce.2.cloned.1.call-update) | async-done | bytes 524304 | tf_op jit(solution)/shard_map/psum | solution.py:85
  699.8 1.9 fusion.70
  701.7 0.8 fusion.78
  702.6 0.8 convolution_multiply_fusion.2
  703.4 0.8 convolution_negate_fusion
  704.3 0.9 fusion.11
  705.1 0.9 fusion.9
  706.1 1.6 copy.108
  707.7 31.5 %all-to-all-start.2 = ((f32[2,128,8,128]{3,2,0,1:T(8,128)}), f32[2,128,8,128]{3,2,0,1:T(8,128)S(1)}, u32[]{:S(2)}, u32[]{:S(2)}) async-start(f32[2,128,8,128]{3,2,0,1:T(8,128)} %copy.108), calls=%async_computation.2 | async-start | bytes 2097152 | tf_op jit(solution)/shard_map/all_to_all | solution.py:92
  739.3 48.5 %all-to-all-done.2 = f32[2,128,8,128]{3,2,0,1:T(8,128)S(1)} async-done(((f32[2,128,8,128]{3,2,0,1:T(8,128)}), f32[2,128,8,128]{3,2,0,1:T(8,128)S(1)}, u32[]{:S(2)}, u32[]{:S(2)}) %all-to-all-start.2) | async-done | bytes 1048608 | tf_op jit(solution)/shard_map/all_to_all | solution.py:92
  787.9 0.8 convolution_multiply_fusion
  788.7 0.8 fusion.35
  789.6 0.9 fusion.8
  790.5 0.8 fusion.74
  791.4 0.8 fusion.47
  792.2 0.9 fusion.5
  793.2 0.9 fusion.3
  794.0 0.9 fusion.2
  795.0 1.6 copy.110
  796.6 6.7 all-to-all-start.3
  803.9 0.6 copy.123
  804.5 47.4 %all-to-all-done.3 = f32[2,8,128,128]{3,1,0,2:T(8,128)S(1)} async-done(((f32[2,8,128,128]{3,1,0,2:T(8,128)}), f32[2,8,128,128]{3,1,0,2:T(8,128)S(1)}, u32[]{:S(2)}, u32[]{:S(2)}) %all-to-all-start.3) | async-done | bytes 1048608 | tf_op jit(solution)/shard_map/all_to_all | solution.py:102
  854.5 1.1 fusion.22
  (29 shorter events, 4.2 us)
Async XLA Ops:
  21.7 61.1 %all-to-all-start = ((f32[2,8,128,128]{3,1,0,2:T(8,128)}), f32[2,8,128,128]{3,1,0,2:T(8,128)S(1)}, u32[]{:S(2)}, u32[]{:S(2)}) async-start(f32[2,8,128,128]{3,1,0,2:T(8,128)} %copy.102), calls=%async_computation | async-start | bytes 2097152 | tf_op jit(solution)/shard_map/all_to_all | solution.py:77
  34.2 55.5 %copy-start.2 = (f32[2]{0:T(128)S(1)}, f32[2]{0:T(128)}, u32[]{:S(2)}) copy-start(f32[2]{0:T(128)} %param.6) | copy-start | bytes 28
  82.8 55.3 %all-to-all-start.1 = ((f32[2,8,128,128]{3,1,0,2:T(8,128)}), f32[2,8,128,128]{3,1,0,2:T(8,128)S(1)}, u32[]{:S(2)}, u32[]{:S(2)}) async-start(f32[2,8,128,128]{3,1,0,2:T(8,128)} %copy.104), calls=%async_computation.1 | async-start | bytes 2097152 | tf_op jit(solution)/shard_map/all_to_all | solution.py:77
  89.5 610.3 %all-reduce.2.cloned.1.call-start = ((), (), s32[]{:S(2)}) async-start(), calls=%async_computation.4 | async-start | bytes 1048576 | tf_op jit(solution)/shard_map/psum | solution.py:85
  699.8 3.6 copy-start
  707.7 80.1 %all-to-all-start.2 = ((f32[2,128,8,128]{3,2,0,1:T(8,128)}), f32[2,128,8,128]{3,2,0,1:T(8,128)S(1)}, u32[]{:S(2)}, u32[]{:S(2)}) async-start(f32[2,128,8,128]{3,2,0,1:T(8,128)} %copy.108), calls=%async_computation.2 | async-start | bytes 2097152 | tf_op jit(solution)/shard_map/all_to_all | solution.py:92
  795.0 8.8 %copy-start.1 = (f32[4,8,128]{2,1,0:T(8,128)S(1)}, f32[4,8,128]{2,1,0:T(8,128)}, u32[]{:S(2)}) copy-start(f32[4,8,128]{2,1,0:T(8,128)} %param.7) | copy-start | bytes 49156
  796.6 55.3 %all-to-all-start.3 = ((f32[2,8,128,128]{3,1,0,2:T(8,128)}), f32[2,8,128,128]{3,1,0,2:T(8,128)S(1)}, u32[]{:S(2)}, u32[]{:S(2)}) async-start(f32[2,8,128,128]{3,1,0,2:T(8,128)} %copy.110), calls=%async_computation.3 | async-start | bytes 2097152 | tf_op jit(solution)/shard_map/all_to_all | solution.py:102
Sparse Core Ops, SparseCore 0:
  145.7 554.0 all-reduce.1
where the time goes:
time: 863 us; the launch traced here: 862 us
  waiting for transfers between devices  743 us (86%)
  starting transfers between devices  57.6 us (7%)
  matrix products  35.4 us (4%)
  between operations  14.4 us (2%)
    psum x1, waiting for transfers between devices, local(): density = lax.psum(partial_value, 'band')  554 us
    all_to_all x2, waiting for transfers between devices, local(): lax.all_to_all(stacked[member], 'slab', split_axis=2, concat_axis=1, tile...  92.9 us
    all_to_all x1, waiting for transfers between devices, local(): lax.all_to_all(jnp.stack((line_real, line_imag)), 'slab', split_axis=1, c...  48.5 us
    all_to_all x1, waiting for transfers between devices, local(): lax.all_to_all(jnp.stack((line_real, line_imag)), 'slab', split_axis=2, c...  47.4 us
    dot_general x36, matrix products, project(): return jnp.einsum(pattern, values, matrix, precision=lax.Precision.HIGHEST)  35.4 us
    all_to_all x1, starting transfers between devices, local(): lax.all_to_all(jnp.stack((line_real, line_imag)), 'slab', split_axis=1, c...  31.5 us
    all_to_all x2, starting transfers between devices, local(): lax.all_to_all(stacked[member], 'slab', split_axis=2, concat_axis=1, tile...  19.2 us
  transfers between devices with their start and end apart: 5, of which 5 were waited for; matrix products, arithmetic and copies ran while one was open for 1% of the time, Pallas kernels for 0%

commit v1 on v0

--- a/solution.py
+++ b/solution.py
@@ -82,7 +82,8 @@
             plane_real * plane_real + plane_imag * plane_imag
         )
     partial_value = partial_value * factor
-    density = lax.psum(partial_value, "band")
+    x_next = lax.all_gather(partial_value, "band")
+    density = jnp.sum(x_next, 0)
     own_density = lax.dynamic_slice_in_dim(density, band_index * band_rows, band_rows, 0)
     first_real = project("xyz,zw->xyw", density, cosine_table)
     first_imag = -project("xyz,zw->xyw", density, sine_table)

time: 863 us -> 723 us (0.84)
  the two profiles are of different devices: /device:TPU:65 before, /device:TPU:71 now
where the time goes in v1:
time: 723 us; the launch traced here: 714 us
  waiting for transfers between devices  612 us (85%)
  matrix products  34.5 us (5%)
  starting transfers between devices  34.5 us (5%)
  between operations  14.6 us (2%)
  other arithmetic  10.6 us (1%)
  local copies, waits for them, and re-layouts  8.38 us (1%)
    all_gather x1, waiting for transfers between devices, local(): x_next = lax.all_gather(partial_value, 'band')  423 us
    all_to_all x2, waiting for transfers between devices, local(): lax.all_to_all(stacked[member], 'slab', split_axis=2, concat_axis=1, tile...  92.7 us
    all_to_all x1, waiting for transfers between devices, local(): lax.all_to_all(jnp.stack((line_real, line_imag)), 'slab', split_axis=1, c...  48.5 us
    all_to_all x1, waiting for transfers between devices, local(): lax.all_to_all(jnp.stack((line_real, line_imag)), 'slab', split_axis=2, c...  47.3 us
    dot_general x36, matrix products, project(): return jnp.einsum(pattern, values, matrix, precision=lax.Precision.HIGHEST)  34.5 us
    all_to_all x2, starting transfers between devices, local(): lax.all_to_all(stacked[member], 'slab', split_axis=2, concat_axis=1, tile...  19.2 us
  transfers between devices with their start and end apart: 5, of which 5 were waited for; matrix products, arithmetic and copies ran while one was open for 1% of the time, Pallas kernels for 0%

profile of v1, /device:TPU:71, one launch (start us, length us, event | category | flops | bytes accessed | tf_op | source)
XLA Modules:
  0.0 714.3 jit_solution(17745551562639735580)
XLA Ops:
  7.2 0.7 dynamic-slice_convert_fusion
  7.9 1.9 copy_multiply_fusion
  9.7 1.2 fusion.26
  11.0 1.2 fusion.27
  12.2 1.2 convolution_subtract_fusion.1
  13.4 1.3 fusion.61
  14.7 1.3 fusion.64
  16.0 1.2 convolution_add_fusion.1
  17.2 1.3 fusion.1
  18.6 1.3 fusion
  20.1 1.6 copy.102
  21.7 12.5 %all-to-all-start = ((f32[2,8,128,128]{3,1,0,2:T(8,128)}), f32[2,8,128,128]{3,1,0,2:T(8,128)S(1)}, u32[]{:S(2)}, u32[]{:S(2)}) async-start(f32[2,8,128,128]{3,1,0,2:T(8,128)} %copy.102), calls=%async_computation | async-start | bytes 2097152 | tf_op jit(solution)/shard_map/all_to_all | solution.py:77
  34.2 1.6 copy.104
  35.8 47.0 %all-to-all-done = f32[2,8,128,128]{3,1,0,2:T(8,128)S(1)} async-done(((f32[2,8,128,128]{3,1,0,2:T(8,128)}), f32[2,8,128,128]{3,1,0,2:T(8,128)S(1)}, u32[]{:S(2)}, u32[]{:S(2)}) %all-to-all-start) | async-done | bytes 1048608 | tf_op jit(solution)/shard_map/all_to_all | solution.py:77
  82.7 6.7 all-to-all-start.1
  90.7 0.8 fusion.32
  91.5 0.8 fusion.31
  92.4 45.7 %all-to-all-done.1 = f32[2,8,128,128]{3,1,0,2:T(8,128)S(1)} async-done(((f32[2,8,128,128]{3,1,0,2:T(8,128)}), f32[2,8,128,128]{3,1,0,2:T(8,128)S(1)}, u32[]{:S(2)}, u32[]{:S(2)}) %all-to-all-start.1) | async-done | bytes 1048608 | tf_op jit(solution)/shard_map/all_to_all | solution.py:77
  138.2 0.8 fusion.34
  139.0 0.8 fusion.33
  139.9 0.9 fusion.16
  140.7 0.9 fusion.20
  141.6 1.6 fusion.19
  143.2 2.4 fusion.21
  145.6 423.3 %all-gather.3.cloned.1.call-done = f32[4096,8,128]{2,0,1:T(8,128)} async-done(((f32[128,8,128]{2,0,1:T(8,128)}), f32[4096,8,128]{2,0,1:T(8,128)}) %all-gather.3.cloned.1.call-update) | async-done | bytes 16777232 | tf_op jit(solution)/shard_map/all_gather | solution.py:85
  568.9 6.9 reduce_sum.9
  575.9 0.8 fusion.70
  576.7 0.8 convolution_negate_fusion
  577.5 0.8 fusion.78
  578.4 0.8 convolution_multiply_fusion.2
  579.2 0.9 fusion.11
  580.1 1.0 fusion.9
  581.2 1.6 copy.108
  582.8 7.8 %all-to-all-start.2 = ((f32[2,128,8,128]{3,2,0,1:T(8,128)}), f32[2,128,8,128]{3,2,0,1:T(8,128)S(1)}, u32[]{:S(2)}, u32[]{:S(2)}) async-start(f32[2,128,8,128]{3,2,0,1:T(8,128)} %copy.108), calls=%async_computation.2 | async-start | bytes 2097152 | tf_op jit(solution)/shard_map/all_to_all | solution.py:93
  590.7 48.5 %all-to-all-done.2 = f32[2,128,8,128]{3,2,0,1:T(8,128)S(1)} async-done(((f32[2,128,8,128]{3,2,0,1:T(8,128)}), f32[2,128,8,128]{3,2,0,1:T(8,128)S(1)}, u32[]{:S(2)}, u32[]{:S(2)}) %all-to-all-start.2) | async-done | bytes 1048608 | tf_op jit(solution)/shard_map/all_to_all | solution.py:93
  639.3 0.8 convolution_multiply_fusion
  640.1 0.8 fusion.35
  641.0 0.9 fusion.8
  641.9 0.8 fusion.74
  642.8 0.8 fusion.47
  643.6 0.9 fusion.5
  644.6 0.9 fusion.3
  645.4 0.9 fusion.2
  646.4 1.6 copy.110
  648.0 7.0 all-to-all-start.3
  655.6 0.6 copy.123
  656.2 47.3 %all-to-all-done.3 = f32[2,8,128,128]{3,1,0,2:T(8,128)S(1)} async-done(((f32[2,8,128,128]{3,1,0,2:T(8,128)}), f32[2,8,128,128]{3,1,0,2:T(8,128)S(1)}, u32[]{:S(2)}, u32[]{:S(2)}) %all-to-all-start.3) | async-done | bytes 1048608 | tf_op jit(solution)/shard_map/all_to_all | solution.py:103
  706.2 1.1 fusion.22
  (28 shorter events, 5.1 us)
Async XLA Ops:
  21.7 61.1 %all-to-all-start = ((f32[2,8,128,128]{3,1,0,2:T(8,128)}), f32[2,8,128,128]{3,1,0,2:T(8,128)S(1)}, u32[]{:S(2)}, u32[]{:S(2)}) async-start(f32[2,8,128,128]{3,1,0,2:T(8,128)} %copy.102), calls=%async_computation | async-start | bytes 2097152 | tf_op jit(solution)/shard_map/all_to_all | solution.py:77
  34.1 55.8 %copy-start.1 = (f32[2]{0:T(128)S(1)}, f32[2]{0:T(128)}, u32[]{:S(2)}) copy-start(f32[2]{0:T(128)} %param.6) | copy-start | bytes 28
  82.7 55.3 %all-to-all-start.1 = ((f32[2,8,128,128]{3,1,0,2:T(8,128)}), f32[2,8,128,128]{3,1,0,2:T(8,128)S(1)}, u32[]{:S(2)}, u32[]{:S(2)}) async-start(f32[2,8,128,128]{3,1,0,2:T(8,128)} %copy.104), calls=%async_computation.1 | async-start | bytes 2097152 | tf_op jit(solution)/shard_map/all_to_all | solution.py:77
  89.5 479.5 %all-gather.3.cloned.1.call-start = ((), (), s32[]{:S(2)}) async-start(), calls=%async_computation.4 | async-start | bytes 17301504 | tf_op jit(solution)/shard_map/all_gather | solution.py:85
  582.8 56.4 %all-to-all-start.2 = ((f32[2,128,8,128]{3,2,0,1:T(8,128)}), f32[2,128,8,128]{3,2,0,1:T(8,128)S(1)}, u32[]{:S(2)}, u32[]{:S(2)}) async-start(f32[2,128,8,128]{3,2,0,1:T(8,128)} %copy.108), calls=%async_computation.2 | async-start | bytes 2097152 | tf_op jit(solution)/shard_map/all_to_all | solution.py:93
  646.4 9.1 %copy-start = (f32[4,8,128]{2,1,0:T(8,128)S(1)}, f32[4,8,128]{2,1,0:T(8,128)}, u32[]{:S(2)}) copy-start(f32[4,8,128]{2,1,0:T(8,128)} %param.7) | copy-start | bytes 49156
  648.0 55.5 %all-to-all-start.3 = ((f32[2,8,128,128]{3,1,0,2:T(8,128)}), f32[2,8,128,128]{3,1,0,2:T(8,128)S(1)}, u32[]{:S(2)}, u32[]{:S(2)}) async-start(f32[2,8,128,128]{3,1,0,2:T(8,128)} %copy.110), calls=%async_computation.3 | async-start | bytes 2097152 | tf_op jit(solution)/shard_map/all_to_all | solution.py:103
Sparse Core Ops, SparseCore 0:
  145.7 423.1 all-gather.2
